TPU v7x, 256 devices: a whole 4x4x8 slice. The times are simulated.
256 devices in a mesh: tm: 16 (over z, core), tile: 16 (over x, y).
Axes of the slice: x: 4, y: 4, z: 8, core: 2. Of those that a mesh axis runs over, the one named last changes fastest.
Arguments:
- obs_values: bfloat16 [16, 32768, 128], P('tm', 'tile'), may hold values from -6 to 6
- obs_weight: bfloat16 [16, 32768, 128], P('tm', 'tile'), may hold values from 0.19921875 to 2
- obs_count: int32 [16, 32768], P('tm', 'tile'), may hold values from 32 to 128
- dest_tile: int32 [16, 32768, 1], P('tm', 'tile'), may hold values from 0 to 15; in each aligned block of 2048 rows (0 to 2047, 2048 to 4095, ..., all dimensions but the last counted through in order) at most 256 rows name the same one
- jac_index: int32 [16, 32768], P('tm', 'tile'), may hold values from 0 to 255
- jacobian: bfloat16 [16, 4096, 128, 128], P('tm', 'tile'), may hold values from -0.5 to 0.5
- jac_state: int32 [16, 4096], P('tm', 'tile'), may hold values from 0 to 63
- corr_blocks: bfloat16 [16, 768, 128, 128], P('tm', 'tile'), may hold values from -0.625 to 0.625
- corr_row: int32 [16, 768], P('tm', 'tile'), may hold values from 0 to 63
- corr_col: int32 [16, 768], P('tm', 'tile'), may hold values from 0 to 63
- time_coupling: bfloat16 [16, 1024, 128], P('tm', 'tile'), may hold values from 0.19921875 to 0.59765625
Outputs:
- product: bfloat16 [16, 32768, 128], P('tm', 'tile')
Inputs may be any that keep to these rules, and one draw needn't show every extreme that they name: `dest_tile`: in the rows of one device, no tile is named by more than 256 observation blocks, a bound that some block reaches.
All inputs are finite; a program needn't handle non-finite values.
Results may differ from a plain program's by a relative error of at most 0.0075.
Values may be sent and summed in bfloat16 or wider, within the bound.
No kernel may reach another device: no remote copies, remote signals or barrier semaphores. Data moves between devices by JAX's collectives and lax.ppermute only.
A program may use at most 64 MiB of HBM per device.

v0:
```python
import jax
import jax.numpy as jnp
from jax import lax
from jax.sharding import PartitionSpec as P


def from_behind(x, axis, by):
    length = lax.axis_size(axis)
    pairs = [(i, i + by) for i in range(length) if 0 <= i + by < length]
    return lax.ppermute(x, axis, pairs)


def shards(
    obs_values,
    obs_weight,
    obs_count,
    dest_tile,
    jac_index,
    jacobian,
    jac_state,
    corr_blocks,
    corr_row,
    corr_col,
    time_coupling,
):
    obs_total = obs_values.shape[1]
    block_width = obs_values.shape[2]
    jac_total = jacobian.shape[1]
    state_total = time_coupling.shape[1]
    lane_index = lax.broadcasted_iota(jnp.int32, (obs_total, block_width), 1)
    keeping = (lane_index < obs_count[0][:, None]).astype(jnp.float32)
    weighted = (
        obs_values[0].astype(jnp.float32) * obs_weight[0].astype(jnp.float32) * keeping
    ).astype(jnp.bfloat16)
    target = dest_tile[0, :, 0]
    column = jac_index[0]
    bin_id = target * jac_total + column
    row_ids = lax.broadcasted_iota(jnp.int32, (jac_total * lax.axis_size("tile"), obs_total), 0)
    picker = (row_ids == bin_id[None, :]).astype(jnp.bfloat16)
    summed = lax.psum_scatter(
        jnp.dot(picker, weighted, preferred_element_type=jnp.float32),
        "tile",
        scatter_dimension=0,
        tiled=True,
    )
    merged = summed.astype(jnp.bfloat16)
    spread = jnp.einsum("kij,ki->kj", jacobian[0], merged, preferred_element_type=jnp.float32)
    state_ids = lax.broadcasted_iota(jnp.int32, (state_total, jac_total), 0)
    owners = state_ids == jac_state[0][None, :]
    state = jnp.dot(owners.astype(jnp.float32), spread, precision=lax.Precision.HIGHEST).astype(
        jnp.bfloat16
    )
    corr_total = corr_blocks.shape[1]
    read_ids = lax.broadcasted_iota(jnp.int32, (corr_total, state_total), 1)
    reader = (read_ids == corr_col[0][:, None]).astype(jnp.bfloat16)
    source = jnp.dot(reader, state, preferred_element_type=jnp.float32).astype(jnp.bfloat16)
    mixing = jnp.einsum("cij,cj->ci", corr_blocks[0], source, preferred_element_type=jnp.float32)
    write_ids = lax.broadcasted_iota(jnp.int32, (state_total, corr_total), 0)
    writer = (write_ids == corr_row[0][None, :]).astype(jnp.float32)
    spatial = jnp.dot(writer, mixing, precision=lax.Precision.HIGHEST).astype(jnp.bfloat16)
    coupling = time_coupling[0]
    earlier = from_behind(spatial, "tm", 1)
    later_state, later_coupling = from_behind((spatial, coupling), "tm", -1)
    coupled = (
        spatial.astype(jnp.float32)
        + coupling.astype(jnp.float32) * earlier.astype(jnp.float32)
        + later_coupling.astype(jnp.float32) * later_state.astype(jnp.float32)
    ).astype(jnp.bfloat16)
    local_state = jnp.dot(
        owners.T.astype(jnp.bfloat16), coupled, preferred_element_type=jnp.float32
    ).astype(jnp.bfloat16)
    model_obs = jnp.einsum(
        "kij,kj->ki", jacobian[0], local_state, preferred_element_type=jnp.float32
    ).astype(jnp.bfloat16)
    portion = lax.all_gather(model_obs, "tile", axis=0, tiled=True)
    columns = lax.broadcasted_iota(jnp.int32, (obs_total, portion.shape[0]), 1)
    picker = (bin_id[:, None] == columns).astype(jnp.bfloat16)
    gathered = jnp.dot(picker, portion, preferred_element_type=jnp.float32)
    return (gathered * keeping).astype(jnp.bfloat16)[None]


def solution(mesh):
    in_specs = (
        P("tm", "tile", None),
        P("tm", "tile", None),
        P("tm", "tile"),
        P("tm", "tile", None),
        P("tm", "tile"),
        P("tm", "tile", None, None),
        P("tm", "tile"),
        P("tm", "tile", None, None),
        P("tm", "tile"),
        P("tm", "tile"),
        P("tm", "tile", None),
    )
    out_specs = P("tm", "tile", None)
    return jax.shard_map(shards, mesh=mesh, in_specs=in_specs, out_specs=out_specs, check_vma=False)
```

profile of v0, /device:TPU:2, one launch (start us, length us, event | category | flops | bytes accessed | tf_op | source)
XLA Modules:
  0.0 185.7 jit_solution(13283383729035749452)
XLA Ops:
  6.5 0.0 copy-start
  6.5 0.0 reduce-scatter.2.cloned.1.call-start
  6.5 0.8 bitcast_add_fusion
  7.4 0.0 copy-start.3
  7.4 8.6 %fusion = f32[4096,128]{1,0:T(8,128)} fusion(s32[2048]{0:T(1024)S(1)} %bitcast.51, bf16[1,2048,128]{2,1,0:T(8,128)(2,1)} %param.12, bf16[1,2048,128]{2,1,0:T(8,128)(2,1)} %param.11, s32[2048]{0:T(1024)} %bitcast.55), kind=kOutput, calls=%fused_computation.2 | convolution fusion | flops 2157445120 | bytes 3162112 | tf_op jit(solution)/shard_map/dot_general | solution.py:41
  16.0 0.0 copy-start.4
  16.0 0.0 copy-start.7
  16.0 0.0 copy-start.5
  16.0 0.0 reduce-scatter.2.cloned.1.call-update
  16.0 0.0 all-gather.2.cloned.1.call-start
  16.1 0.0 copy-done.3
  16.1 1.3 collective-permute-start.1
  17.4 81.6 %reduce-scatter.2.cloned.1.call-done = f32[256,128]{1,0:T(8,128)} async-done(((f32[4096,128]{1,0:T(8,128)}), f32[256,128]{1,0:T(8,128)}) %reduce-scatter.2.cloned.1.call-update) | async-done | bytes 131088 | tf_op jit(solution)/shard_map/reduce_scatter | solution.py:40
  99.0 0.9 convert_bitcast_fusion
  99.9 0.0 copy-start.2
  99.9 0.0 copy-start.1
  99.9 0.0 copy-start.6
  99.9 5.7 %fusion.6 = f32[256,1,128]{2,1,0:T(1,128)S(1)} fusion(bf16[1,256,128,128]{3,2,1,0:T(8,128)(2,1)} %param.16, bf16[256,128,1]{1,0,2:T(8,128)(2,1)S(1)} %convert_bitcast_fusion), kind=kOutput, calls=%fused_computation.8 | convolution fusion | flops 8388608 | bytes 8585216 | tf_op jit(solution)/shard_map/kij,ki->kj/dot_general | solution.py:47
  105.6 0.0 copy-done.4
  105.6 0.2 convolution_convert_fusion.2
  105.8 0.0 copy-done.7
  105.8 0.2 fusion.14
  106.0 0.0 copy-done
  106.0 0.9 fusion.11
  106.9 0.0 copy-done.5
  106.9 0.2 convolution_convert_fusion.1
  107.1 1.3 collective-permute-start
  108.4 1.5 collective-permute-start.2
  109.9 0.0 collective-permute-done.1
  109.9 0.0 collective-permute-done
  109.9 3.4 %collective-permute-done.2 = bf16[64,128]{1,0:T(8,128)(2,1)S(1)} collective-permute-done((bf16[64,128]{1,0:T(8,128)(2,1)S(1)}, bf16[64,128]{1,0:T(8,128)(2,1)S(1)}, u32[]{:S(2)}, u32[]{:S(2)}) %collective-permute-start.2) | collective-permute-done | bytes 16416 | tf_op jit(solution)/shard_map/ppermute | solution.py:10
  113.3 0.2 fusion.13
  113.5 7.8 %fusion.4 = f32[256,1,128]{2,1,0:T(1,128)S(1)} fusion(bf16[1,256,128,128]{3,2,1,0:T(8,128)(2,1)} %param.16, bf16[256,128,1]{1,0,2:T(8,128)(2,1)S(1)} %fusion.13), kind=kOutput, calls=%fused_computation.6 | convolution fusion | flops 8388608 | bytes 8585216 | tf_op jit(solution)/shard_map/kij,kj->ki/dot_general | solution.py:72
  121.3 0.7 convert_element_type.71
  121.9 0.0 all-gather.2.cloned.1.call-update
  121.9 0.0 copy-done.2
  122.0 0.0 copy-done.1
  122.0 49.3 %all-gather.2.cloned.1.call-done = bf16[4096,128]{1,0:T(8,128)(2,1)} async-done(((bf16[256,128]{1,0:T(8,128)(2,1)}), bf16[4096,128]{1,0:T(8,128)(2,1)}) %all-gather.2.cloned.1.call-update) | async-done | bytes 1048592 | tf_op jit(solution)/shard_map/all_gather | solution.py:75
  171.3 0.0 copy-done.6
  171.3 7.6 %fusion.10 = bf16[1,2048,128]{2,1,0:T(8,128)(2,1)} fusion(bf16[4096,128]{1,0:T(8,128)(2,1)} %all-gather.2.cloned.1.call-done, s32[2048]{0:T(1024)S(1)} %add.18, s32[2048]{0:T(1024)S(1)} %bitcast.56), kind=kOutput, calls=%fused_computation.12 | convolution fusion | flops 2156658688 | bytes 1589248 | tf_op jit(solution)/shard_map/dot_general | solution.py:78
  (2 shorter events, 0.0 us)
Async XLA Ops:
  6.5 99.5 %copy-start = (bf16[1,48,128,128]{3,2,1,0:T(8,128)(2,1)S(1)}, bf16[1,48,128,128]{3,2,1,0:T(8,128)(2,1)}, u32[]{:S(2)}) copy-start(bf16[1,48,128,128]{3,2,1,0:T(8,128)(2,1)} %param.18) | copy-start | bytes 4718596
  6.5 92.5 %reduce-scatter.2.cloned.1.call-start = ((), (), s32[]{:S(2)}) async-start(), calls=%async_computation.1 | async-start | bytes 2228224 | tf_op jit(solution)/shard_map/reduce_scatter | solution.py:40
  7.4 8.7 %copy-start.3 = (bf16[1,64,128]{2,1,0:T(8,128)(2,1)S(1)}, bf16[1,64,128]{2,1,0:T(8,128)(2,1)}, u32[]{:S(2)}) copy-start(bf16[1,64,128]{2,1,0:T(8,128)(2,1)} %param.21) | copy-start | bytes 49156
  16.0 89.6 %copy-start.4 = (s32[1,256]{1,0:T(1,128)S(1)}, s32[1,256]{1,0:T(1,128)}, u32[]{:S(2)}) copy-start(s32[1,256]{1,0:T(1,128)} %param.17) | copy-start | bytes 3076
  16.0 89.8 %copy-start.7 = (s32[1,48]{1,0:T(1,128)S(1)}, s32[1,48]{1,0:T(1,128)}, u32[]{:S(2)}) copy-start(s32[1,48]{1,0:T(1,128)} %param.20) | copy-start | bytes 580
  16.0 90.9 %copy-start.5 = (s32[1,48]{1,0:T(1,128)S(1)}, s32[1,48]{1,0:T(1,128)}, u32[]{:S(2)}) copy-start(s32[1,48]{1,0:T(1,128)} %param.19) | copy-start | bytes 580
  16.0 155.3 %all-gather.2.cloned.1.call-start = ((), (), s32[]{:S(2)}) async-start(), calls=%async_computation.2 | async-start | bytes 1114112 | tf_op jit(solution)/shard_map/all_gather | solution.py:75
  16.1 93.8 %collective-permute-start.1 = (bf16[64,128]{1,0:T(8,128)(2,1)S(1)}, bf16[64,128]{1,0:T(8,128)(2,1)S(1)}, u32[]{:S(2)}, u32[]{:S(2)}) collective-permute-start(bf16[64,128]{1,0:T(8,128)(2,1)S(1)} %bitcast.50), channel_id=1, source_target_pairs={{16,0},{32,16},{48,32},{64,48},{80,64},{96,80},{112,96},{128,112},... | collective-permute-start | bytes 49160 | tf_op jit(solution)/shard_map/ppermute | solution.py:10
  99.9 22.0 %copy-start.2 = (s32[1,2048,1]{1,2,0:T(1,128)S(1)}, s32[1,2048,1]{1,2,0:T(1,128)}, u32[]{:S(2)}) copy-start(s32[1,2048,1]{1,2,0:T(1,128)} %param.14) | copy-start | bytes 24580
  99.9 22.1 %copy-start.1 = (s32[1,2048]{1,0:T(1,128)S(1)}, s32[1,2048]{1,0:T(1,128)}, u32[]{:S(2)}) copy-start(s32[1,2048]{1,0:T(1,128)} %param.15) | copy-start | bytes 24580
  99.9 71.4 %copy-start.6 = (s32[1,2048]{1,0:T(1,128)S(1)}, s32[1,2048]{1,0:T(1,128)}, u32[]{:S(2)}) copy-start(s32[1,2048]{1,0:T(1,128)} %param.13) | copy-start | bytes 24580
  107.1 2.8 %collective-permute-start = (bf16[64,128]{1,0:T(8,128)(2,1)S(1)}, bf16[64,128]{1,0:T(8,128)(2,1)S(1)}, u32[]{:S(2)}, u32[]{:S(2)}) collective-permute-start(bf16[64,128]{1,0:T(8,128)(2,1)S(1)} %convolution_convert_fusion.1), channel_id=1, source_target_pairs={{0,16},{16,32},{32,48},{48,64},{64,80},{80,96},{96,112},{112,128},... | collective-permute-start | bytes 49160 | tf_op jit(solution)/shard_map/ppermute | solution.py:10
  108.4 4.9 %collective-permute-start.2 = (bf16[64,128]{1,0:T(8,128)(2,1)S(1)}, bf16[64,128]{1,0:T(8,128)(2,1)S(1)}, u32[]{:S(2)}, u32[]{:S(2)}) collective-permute-start(bf16[64,128]{1,0:T(8,128)(2,1)S(1)} %convolution_convert_fusion.1), channel_id=1, source_target_pairs={{16,0},{32,16},{48,32},{64,48},{80,64},{96,80},{112,96},{128,112},... | collective-permute-start | bytes 49160 | tf_op jit(solution)/shard_map/ppermute | solution.py:10
Sparse Core Ops, SparseCore 0:
  16.1 82.8 reduce-scatter.1
  122.1 49.1 all-gather.1
where the time goes:
time: 186 us
  waiting for transfers between devices  134 us (72%)
  matrix products  31.3 us (17%)
  between operations  13.5 us (7%)
  starting transfers between devices  4.1 us (2%)
  other arithmetic  2.44 us (1%)
    reduce_scatter x1, waiting for transfers between devices, shards(): lax.psum_scatter(jnp.dot(picker, weighted, preferred_element_type=jnp.flo...  81.6 us
    all_gather x1, waiting for transfers between devices, shards(): portion = lax.all_gather(model_obs, 'tile', axis=0, tiled=True)  49.3 us
    dot_general x1, matrix products, shards(): jnp.dot(picker, weighted, preferred_element_type=jnp.float32)  8.59 us
    dot_general x1, matrix products, shards(): jnp.einsum('kij,kj->ki', jacobian[0], local_state, preferred_element_type...  7.78 us
    dot_general x1, matrix products, shards(): gathered = jnp.dot(picker, portion, preferred_element_type=jnp.float32)  7.57 us
    dot_general x1, matrix products, shards(): jnp.einsum('kij,ki->kj', jacobian[0], merged, preferred_element_type=jnp....  5.66 us
    ppermute x3, starting transfers between devices, from_behind(): return lax.ppermute(x, axis, pairs)  4.06 us
  transfers between devices with their start and end apart: 5, of which 3 were waited for; matrix products, arithmetic and copies ran while one was open for 4% of the time, Pallas kernels for 0%

commit v1 on v0

--- a/solution.py
+++ b/solution.py
@@ -23,6 +23,33 @@
     corr_col,
     time_coupling,
 ):
+
+    def track_windows(comm_axis, block_here):
+        last, tile_out, high = (
+            jax.lax.axis_size(comm_axis),
+            jax.lax.axis_index(comm_axis),
+            block_here.shape[0],
+        )
+        log = list(map(lambda p: (p, (p + 1) % last), range(last)))
+        rows = list(map(lambda p: (p, (p - 1) % last), range(last)))
+        piece_out = jnp.zeros(
+            (*block_here.shape[:0], last * high, *block_here.shape[1:]), block_here.dtype
+        )
+        piece_out = lax.dynamic_update_slice_in_dim(piece_out, block_here, tile_out * high, axis=0)
+        t1 = current_arr = block_here
+        main = last // 2
+        for num in tuple(range(1, main + 1)):
+            t1 = jax.lax.ppermute(t1, axis_name=comm_axis, perm=log)
+            piece_out = lax.dynamic_update_slice_in_dim(
+                piece_out, t1, (tile_out - num) % last * high, axis=0
+            )
+            if num < last - main:
+                current_arr = jax.lax.ppermute(current_arr, axis_name=comm_axis, perm=rows)
+                piece_out = lax.dynamic_update_slice_in_dim(
+                    piece_out, current_arr, (tile_out + num) % last * high, axis=0
+                )
+        return piece_out
+
     obs_total = obs_values.shape[1]
     block_width = obs_values.shape[2]
     jac_total = jacobian.shape[1]
@@ -72,7 +99,7 @@
     model_obs = jnp.einsum(
         "kij,kj->ki", jacobian[0], local_state, preferred_element_type=jnp.float32
     ).astype(jnp.bfloat16)
-    portion = lax.all_gather(model_obs, "tile", axis=0, tiled=True)
+    portion = track_windows("tile", block_here=model_obs)
     columns = lax.broadcasted_iota(jnp.int32, (obs_total, portion.shape[0]), 1)
     picker = (bin_id[:, None] == columns).astype(jnp.bfloat16)
     gathered = jnp.dot(picker, portion, preferred_element_type=jnp.float32)

time: 186 us -> 198 us (1.065)
  the two profiles are of different devices: /device:TPU:2 before, /device:TPU:32 now
where the time goes in v1:
time: 198 us; the launch traced here: 197 us
  waiting for transfers between devices  105 us (53%)
  starting transfers between devices  45.6 us (23%)
  matrix products  30.7 us (16%)
  between operations  13.9 us (7%)
    reduce_scatter x1, waiting for transfers between devices, shards(): lax.psum_scatter(jnp.dot(picker, weighted, preferred_element_type=jnp.flo...  80.8 us
    ppermute x7, starting transfers between devices, track_windows(): current_arr = jax.lax.ppermute(current_arr, axis_name=comm_axis, perm=rows)  36.7 us
    ppermute x8, waiting for transfers between devices, track_windows(): t1 = jax.lax.ppermute(t1, axis_name=comm_axis, perm=log)  22.6 us
    dot_general x1, matrix products, shards(): jnp.dot(picker, weighted, preferred_element_type=jnp.float32)  8.57 us
    dot_general x1, matrix products, shards(): jnp.einsum('kij,kj->ki', jacobian[0], local_state, preferred_element_type...  7.78 us
    ppermute x3, starting transfers between devices, from_behind(): return lax.ppermute(x, axis, pairs)  7.61 us
    dot_general x1, matrix products, shards(): gathered = jnp.dot(picker, portion, preferred_element_type=jnp.float32)  7.01 us
    dot_general x1, matrix products, shards(): jnp.einsum('kij,ki->kj', jacobian[0], merged, preferred_element_type=jnp....  5.65 us
  transfers between devices with their start and end apart: 19, of which 10 were waited for; matrix products, arithmetic and copies ran while one was open for 4% of the time, Pallas kernels for 0%

profile of v1, /device:TPU:32, one launch (start us, length us, event | category | flops | bytes accessed | tf_op | source)
XLA Modules:
  0.0 197.3 jit_solution(16818959264797003915)
XLA Ops:
  6.5 0.8 bitcast_add_fusion
  7.4 0.0 copy-start.3
  7.4 8.6 %fusion = f32[4096,128]{1,0:T(8,128)} fusion(s32[2048]{0:T(1024)S(1)} %bitcast.51, bf16[1,2048,128]{2,1,0:T(8,128)(2,1)} %param.12, bf16[1,2048,128]{2,1,0:T(8,128)(2,1)} %param.11, s32[2048]{0:T(1024)} %bitcast.55), kind=kOutput, calls=%fused_computation.2 | convolution fusion | flops 2157445120 | bytes 3162112 | tf_op jit(solution)/shard_map/dot_general | solution.py:68
  16.0 0.0 reduce-scatter.2.cloned.1.call-update
  16.0 2.1 %collective-permute-start.1 = (bf16[64,128]{1,0:T(8,128)(2,1)S(1)}, bf16[64,128]{1,0:T(8,128)(2,1)S(1)}, u32[]{:S(2)}, u32[]{:S(2)}) collective-permute-start(bf16[64,128]{1,0:T(8,128)(2,1)S(1)} %bitcast.50), channel_id=1, source_target_pairs={{16,0},{32,16},{48,32},{64,48},{80,64},{96,80},{112,96},{128,112},... | collective-permute-start | bytes 49160 | tf_op jit(solution)/shard_map/ppermute | solution.py:10
  18.1 80.8 %reduce-scatter.2.cloned.1.call-done = f32[256,128]{1,0:T(8,128)} async-done(((f32[4096,128]{1,0:T(8,128)}), f32[256,128]{1,0:T(8,128)}) %reduce-scatter.2.cloned.1.call-update) | async-done | bytes 131088 | tf_op jit(solution)/shard_map/reduce_scatter | solution.py:67
  98.9 0.9 convert_bitcast_fusion
  99.8 5.7 %fusion.6 = f32[256,1,128]{2,1,0:T(1,128)S(1)} fusion(bf16[1,256,128,128]{3,2,1,0:T(8,128)(2,1)} %param.16, bf16[256,128,1]{1,0,2:T(8,128)(2,1)S(1)} %convert_bitcast_fusion), kind=kOutput, calls=%fused_computation.8 | convolution fusion | flops 8388608 | bytes 8585216 | tf_op jit(solution)/shard_map/kij,ki->kj/dot_general | solution.py:74
  105.5 0.2 convolution_convert_fusion.2
  105.7 0.2 fusion.14
  105.9 0.9 fusion.11
  106.8 0.2 convolution_convert_fusion.1
  107.0 1.9 collective-permute-start
  108.9 3.6 %collective-permute-start.2 = (bf16[64,128]{1,0:T(8,128)(2,1)S(1)}, bf16[64,128]{1,0:T(8,128)(2,1)S(1)}, u32[]{:S(2)}, u32[]{:S(2)}) collective-permute-start(bf16[64,128]{1,0:T(8,128)(2,1)S(1)} %convolution_convert_fusion.1), channel_id=1, source_target_pairs={{16,0},{32,16},{48,32},{64,48},{80,64},{96,80},{112,96},{128,112},... | collective-permute-start | bytes 49160 | tf_op jit(solution)/shard_map/ppermute | solution.py:10
  112.6 0.0 collective-permute-done.1
  112.6 0.0 collective-permute-done
  112.6 1.4 collective-permute-done.2
  114.0 0.2 fusion.13
  114.2 7.8 %fusion.4 = f32[256,1,128]{2,1,0:T(1,128)S(1)} fusion(bf16[1,256,128,128]{3,2,1,0:T(8,128)(2,1)} %param.16, bf16[256,128,1]{1,0,2:T(8,128)(2,1)S(1)} %fusion.13), kind=kOutput, calls=%fused_computation.6 | convolution fusion | flops 8388608 | bytes 8585216 | tf_op jit(solution)/shard_map/kij,kj->ki/dot_general | solution.py:99
  122.0 0.2 broadcast_in_dim.8
  122.2 1.3 collective-permute-start.3
  123.5 4.2 %collective-permute-start.4 = (bf16[256,128]{1,0:T(8,128)(2,1)S(1)}, bf16[256,128]{1,0:T(8,128)(2,1)S(1)}, u32[]{:S(2)}, u32[]{:S(2)}) collective-permute-start(bf16[256,128]{1,0:T(8,128)(2,1)S(1)} %get-tuple-element.6), channel_id=1, source_target_pairs={{0,15},{1,0},{2,1},{3,2},{4,3},{5,4},{6,5},{7,6},{8,7},{9,8},{10,9... | collective-permute-start | bytes 196616 | tf_op jit(solution)/shard_map/ppermute | solution.py:47
  127.9 2.0 collective-permute-done.3
  129.9 0.0 collective-permute-start.5
  129.9 0.0 collective-permute-done.4
  129.9 5.6 %collective-permute-start.6 = (bf16[256,128]{1,0:T(8,128)(2,1)S(1)}, bf16[256,128]{1,0:T(8,128)(2,1)S(1)}, u32[]{:S(2)}, u32[]{:S(2)}) collective-permute-start(bf16[256,128]{1,0:T(8,128)(2,1)S(1)} %collective-permute-done.4), channel_id=1, source_target_pairs={{0,15},{1,0},{2,1},{3,2},{4,3},{5,4},{6,5},{7,6},{8,7},{9,8},{10,9... | collective-permute-start | bytes 196616 | tf_op jit(solution)/shard_map/ppermute | solution.py:47
  135.5 2.1 %collective-permute-done.5 = bf16[256,128]{1,0:T(8,128)(2,1)S(1)} collective-permute-done((bf16[256,128]{1,0:T(8,128)(2,1)S(1)}, bf16[256,128]{1,0:T(8,128)(2,1)S(1)}, u32[]{:S(2)}, u32[]{:S(2)}) %collective-permute-start.5) | collective-permute-done | bytes 65568 | tf_op jit(solution)/shard_map/ppermute | solution.py:42
  137.7 0.0 collective-permute-start.7
  137.7 0.0 collective-permute-done.6
  137.7 5.4 %collective-permute-start.8 = (bf16[256,128]{1,0:T(8,128)(2,1)S(1)}, bf16[256,128]{1,0:T(8,128)(2,1)S(1)}, u32[]{:S(2)}, u32[]{:S(2)}) collective-permute-start(bf16[256,128]{1,0:T(8,128)(2,1)S(1)} %collective-permute-done.6), channel_id=1, source_target_pairs={{0,15},{1,0},{2,1},{3,2},{4,3},{5,4},{6,5},{7,6},{8,7},{9,8},{10,9... | collective-permute-start | bytes 196616 | tf_op jit(solution)/shard_map/ppermute | solution.py:47
  143.1 2.1 %collective-permute-done.7 = bf16[256,128]{1,0:T(8,128)(2,1)S(1)} collective-permute-done((bf16[256,128]{1,0:T(8,128)(2,1)S(1)}, bf16[256,128]{1,0:T(8,128)(2,1)S(1)}, u32[]{:S(2)}, u32[]{:S(2)}) %collective-permute-start.7) | collective-permute-done | bytes 65568 | tf_op jit(solution)/shard_map/ppermute | solution.py:42
  145.3 0.0 collective-permute-start.9
  145.3 0.0 collective-permute-done.8
  145.3 5.4 %collective-permute-start.10 = (bf16[256,128]{1,0:T(8,128)(2,1)S(1)}, bf16[256,128]{1,0:T(8,128)(2,1)S(1)}, u32[]{:S(2)}, u32[]{:S(2)}) collective-permute-start(bf16[256,128]{1,0:T(8,128)(2,1)S(1)} %collective-permute-done.8), channel_id=1, source_target_pairs={{0,15},{1,0},{2,1},{3,2},{4,3},{5,4},{6,5},{7,6},{8,7},{9,8},{10,9... | collective-permute-start | bytes 196616 | tf_op jit(solution)/shard_map/ppermute | solution.py:47
  150.7 2.1 %collective-permute-done.9 = bf16[256,128]{1,0:T(8,128)(2,1)S(1)} collective-permute-done((bf16[256,128]{1,0:T(8,128)(2,1)S(1)}, bf16[256,128]{1,0:T(8,128)(2,1)S(1)}, u32[]{:S(2)}, u32[]{:S(2)}) %collective-permute-start.9) | collective-permute-done | bytes 65568 | tf_op jit(solution)/shard_map/ppermute | solution.py:42
  152.9 0.0 collective-permute-start.11
  152.9 0.0 collective-permute-done.10
  152.9 5.4 %collective-permute-start.12 = (bf16[256,128]{1,0:T(8,128)(2,1)S(1)}, bf16[256,128]{1,0:T(8,128)(2,1)S(1)}, u32[]{:S(2)}, u32[]{:S(2)}) collective-permute-start(bf16[256,128]{1,0:T(8,128)(2,1)S(1)} %collective-permute-done.10), channel_id=1, source_target_pairs={{0,15},{1,0},{2,1},{3,2},{4,3},{5,4},{6,5},{7,6},{8,7},{9,8},{10,9... | collective-permute-start | bytes 196616 | tf_op jit(solution)/shard_map/ppermute | solution.py:47
  158.3 2.1 %collective-permute-done.11 = bf16[256,128]{1,0:T(8,128)(2,1)S(1)} collective-permute-done((bf16[256,128]{1,0:T(8,128)(2,1)S(1)}, bf16[256,128]{1,0:T(8,128)(2,1)S(1)}, u32[]{:S(2)}, u32[]{:S(2)}) %collective-permute-start.11) | collective-permute-done | bytes 65568 | tf_op jit(solution)/shard_map/ppermute | solution.py:42
  160.5 0.0 collective-permute-start.13
  160.5 0.0 collective-permute-done.12
  160.5 5.4 %collective-permute-start.14 = (bf16[256,128]{1,0:T(8,128)(2,1)S(1)}, bf16[256,128]{1,0:T(8,128)(2,1)S(1)}, u32[]{:S(2)}, u32[]{:S(2)}) collective-permute-start(bf16[256,128]{1,0:T(8,128)(2,1)S(1)} %collective-permute-done.12), channel_id=1, source_target_pairs={{0,15},{1,0},{2,1},{3,2},{4,3},{5,4},{6,5},{7,6},{8,7},{9,8},{10,9... | collective-permute-start | bytes 196616 | tf_op jit(solution)/shard_map/ppermute | solution.py:47
  165.9 2.1 %collective-permute-done.13 = bf16[256,128]{1,0:T(8,128)(2,1)S(1)} collective-permute-done((bf16[256,128]{1,0:T(8,128)(2,1)S(1)}, bf16[256,128]{1,0:T(8,128)(2,1)S(1)}, u32[]{:S(2)}, u32[]{:S(2)}) %collective-permute-start.13) | collective-permute-done | bytes 65568 | tf_op jit(solution)/shard_map/ppermute | solution.py:42
  168.0 0.0 collective-permute-done.14
  168.0 5.4 %collective-permute-start.16 = (bf16[256,128]{1,0:T(8,128)(2,1)S(1)}, bf16[256,128]{1,0:T(8,128)(2,1)S(1)}, u32[]{:S(2)}, u32[]{:S(2)}) collective-permute-start(bf16[256,128]{1,0:T(8,128)(2,1)S(1)} %collective-permute-done.14), channel_id=1, source_target_pairs={{0,15},{1,0},{2,1},{3,2},{4,3},{5,4},{6,5},{7,6},{8,7},{9,8},{10,9... | collective-permute-start | bytes 196616 | tf_op jit(solution)/shard_map/ppermute | solution.py:47
  173.5 2.3 %collective-permute-done.15 = bf16[256,128]{1,0:T(8,128)(2,1)S(1)} collective-permute-done((bf16[256,128]{1,0:T(8,128)(2,1)S(1)}, bf16[256,128]{1,0:T(8,128)(2,1)S(1)}, u32[]{:S(2)}, u32[]{:S(2)}) %collective-permute-start.15) | collective-permute-done | bytes 65568 | tf_op jit(solution)/shard_map/ppermute | solution.py:42
  175.9 7.5 %collective-permute-done.17 = bf16[256,128]{1,0:T(8,128)(2,1)S(1)} collective-permute-done((bf16[256,128]{1,0:T(8,128)(2,1)S(1)}, bf16[256,128]{1,0:T(8,128)(2,1)S(1)}, u32[]{:S(2)}, u32[]{:S(2)}) %collective-permute-start.17) | collective-permute-done | bytes 65568 | tf_op jit(solution)/shard_map/ppermute | solution.py:42
  183.4 7.0 %fusion.10 = bf16[1,2048,128]{2,1,0:T(8,128)(2,1)} fusion(bf16[4096,128]{1,0:T(8,128)(2,1)S(1)} %constant_dynamic-update-slice_fusion, s32[2048]{0:T(1024)S(1)} %add.141, s32[2048]{0:T(1024)S(1)} %bitcast.56), kind=kOutput, calls=%fused_computation.12 | convolution fusion | flops 2156658688 | bytes 1589248 | tf_op jit(solution)/shard_map/dot_general | solution.py:105
  (37 shorter events, 0.3 us)
Async XLA Ops:
  6.5 99.4 %copy-start = (bf16[1,48,128,128]{3,2,1,0:T(8,128)(2,1)S(1)}, bf16[1,48,128,128]{3,2,1,0:T(8,128)(2,1)}, u32[]{:S(2)}) copy-start(bf16[1,48,128,128]{3,2,1,0:T(8,128)(2,1)} %param.18) | copy-start | bytes 4718596
  6.5 92.4 %reduce-scatter.2.cloned.1.call-start = ((), (), s32[]{:S(2)}) async-start(), calls=%async_computation.1 | async-start | bytes 2228224 | tf_op jit(solution)/shard_map/reduce_scatter | solution.py:67
  7.4 8.6 %copy-start.3 = (bf16[1,64,128]{2,1,0:T(8,128)(2,1)S(1)}, bf16[1,64,128]{2,1,0:T(8,128)(2,1)}, u32[]{:S(2)}) copy-start(bf16[1,64,128]{2,1,0:T(8,128)(2,1)} %param.21) | copy-start | bytes 49156
  16.0 89.5 %copy-start.4 = (s32[1,256]{1,0:T(1,128)S(1)}, s32[1,256]{1,0:T(1,128)}, u32[]{:S(2)}) copy-start(s32[1,256]{1,0:T(1,128)} %param.17) | copy-start | bytes 3076
  16.0 89.7 %copy-start.7 = (s32[1,48]{1,0:T(1,128)S(1)}, s32[1,48]{1,0:T(1,128)}, u32[]{:S(2)}) copy-start(s32[1,48]{1,0:T(1,128)} %param.20) | copy-start | bytes 580
  16.0 90.8 %copy-start.5 = (s32[1,48]{1,0:T(1,128)S(1)}, s32[1,48]{1,0:T(1,128)}, u32[]{:S(2)}) copy-start(s32[1,48]{1,0:T(1,128)} %param.19) | copy-start | bytes 580
  16.0 96.6 %collective-permute-start.1 = (bf16[64,128]{1,0:T(8,128)(2,1)S(1)}, bf16[64,128]{1,0:T(8,128)(2,1)S(1)}, u32[]{:S(2)}, u32[]{:S(2)}) collective-permute-start(bf16[64,128]{1,0:T(8,128)(2,1)S(1)} %bitcast.50), channel_id=1, source_target_pairs={{16,0},{32,16},{48,32},{64,48},{80,64},{96,80},{112,96},{128,112},... | collective-permute-start | bytes 49160 | tf_op jit(solution)/shard_map/ppermute | solution.py:10
  99.8 27.8 %copy-start.2 = (s32[1,2048,1]{1,2,0:T(1,128)S(1)}, s32[1,2048,1]{1,2,0:T(1,128)}, u32[]{:S(2)}) copy-start(s32[1,2048,1]{1,2,0:T(1,128)} %param.14) | copy-start | bytes 24580
  105.5 22.4 %copy-start.1 = (s32[1,2048]{1,0:T(1,128)S(1)}, s32[1,2048]{1,0:T(1,128)}, u32[]{:S(2)}) copy-start(s32[1,2048]{1,0:T(1,128)} %param.15) | copy-start | bytes 24580
  105.5 77.9 %copy-start.6 = (s32[1,2048]{1,0:T(1,128)S(1)}, s32[1,2048]{1,0:T(1,128)}, u32[]{:S(2)}) copy-start(s32[1,2048]{1,0:T(1,128)} %param.13) | copy-start | bytes 24580
  107.0 5.6 %collective-permute-start = (bf16[64,128]{1,0:T(8,128)(2,1)S(1)}, bf16[64,128]{1,0:T(8,128)(2,1)S(1)}, u32[]{:S(2)}, u32[]{:S(2)}) collective-permute-start(bf16[64,128]{1,0:T(8,128)(2,1)S(1)} %convolution_convert_fusion.1), channel_id=1, source_target_pairs={{0,16},{16,32},{32,48},{48,64},{64,80},{80,96},{96,112},{112,128},... | collective-permute-start | bytes 49160 | tf_op jit(solution)/shard_map/ppermute | solution.py:10
  108.9 5.1 %collective-permute-start.2 = (bf16[64,128]{1,0:T(8,128)(2,1)S(1)}, bf16[64,128]{1,0:T(8,128)(2,1)S(1)}, u32[]{:S(2)}, u32[]{:S(2)}) collective-permute-start(bf16[64,128]{1,0:T(8,128)(2,1)S(1)} %convolution_convert_fusion.1), channel_id=1, source_target_pairs={{16,0},{32,16},{48,32},{64,48},{80,64},{96,80},{112,96},{128,112},... | collective-permute-start | bytes 49160 | tf_op jit(solution)/shard_map/ppermute | solution.py:10
  122.2 7.7 %collective-permute-start.3 = (bf16[256,128]{1,0:T(8,128)(2,1)S(1)}, bf16[256,128]{1,0:T(8,128)(2,1)S(1)}, u32[]{:S(2)}, u32[]{:S(2)}) collective-permute-start(bf16[256,128]{1,0:T(8,128)(2,1)S(1)} %get-tuple-element.6), channel_id=1, source_target_pairs={{0,1},{1,2},{2,3},{3,4},{4,5},{5,6},{6,7},{7,8},{8,9},{9,10},{10,1... | collective-permute-start | bytes 196616 | tf_op jit(solution)/shard_map/ppermute | solution.py:42
  123.5 6.4 %collective-permute-start.4 = (bf16[256,128]{1,0:T(8,128)(2,1)S(1)}, bf16[256,128]{1,0:T(8,128)(2,1)S(1)}, u32[]{:S(2)}, u32[]{:S(2)}) collective-permute-start(bf16[256,128]{1,0:T(8,128)(2,1)S(1)} %get-tuple-element.6), channel_id=1, source_target_pairs={{0,15},{1,0},{2,1},{3,2},{4,3},{5,4},{6,5},{7,6},{8,7},{9,8},{10,9... | collective-permute-start | bytes 196616 | tf_op jit(solution)/shard_map/ppermute | solution.py:47
  129.9 7.8 %collective-permute-start.5 = (bf16[256,128]{1,0:T(8,128)(2,1)S(1)}, bf16[256,128]{1,0:T(8,128)(2,1)S(1)}, u32[]{:S(2)}, u32[]{:S(2)}) collective-permute-start(bf16[256,128]{1,0:T(8,128)(2,1)S(1)} %collective-permute-done.3), channel_id=1, source_target_pairs={{0,1},{1,2},{2,3},{3,4},{4,5},{5,6},{6,7},{7,8},{8,9},{9,10},{10,1... | collective-permute-start | bytes 196616 | tf_op jit(solution)/shard_map/ppermute | solution.py:42
  129.9 7.8 %collective-permute-start.6 = (bf16[256,128]{1,0:T(8,128)(2,1)S(1)}, bf16[256,128]{1,0:T(8,128)(2,1)S(1)}, u32[]{:S(2)}, u32[]{:S(2)}) collective-permute-start(bf16[256,128]{1,0:T(8,128)(2,1)S(1)} %collective-permute-done.4), channel_id=1, source_target_pairs={{0,15},{1,0},{2,1},{3,2},{4,3},{5,4},{6,5},{7,6},{8,7},{9,8},{10,9... | collective-permute-start | bytes 196616 | tf_op jit(solution)/shard_map/ppermute | solution.py:47
  137.7 7.6 %collective-permute-start.7 = (bf16[256,128]{1,0:T(8,128)(2,1)S(1)}, bf16[256,128]{1,0:T(8,128)(2,1)S(1)}, u32[]{:S(2)}, u32[]{:S(2)}) collective-permute-start(bf16[256,128]{1,0:T(8,128)(2,1)S(1)} %collective-permute-done.5), channel_id=1, source_target_pairs={{0,1},{1,2},{2,3},{3,4},{4,5},{5,6},{6,7},{7,8},{8,9},{9,10},{10,1... | collective-permute-start | bytes 196616 | tf_op jit(solution)/shard_map/ppermute | solution.py:42
  137.7 7.6 %collective-permute-start.8 = (bf16[256,128]{1,0:T(8,128)(2,1)S(1)}, bf16[256,128]{1,0:T(8,128)(2,1)S(1)}, u32[]{:S(2)}, u32[]{:S(2)}) collective-permute-start(bf16[256,128]{1,0:T(8,128)(2,1)S(1)} %collective-permute-done.6), channel_id=1, source_target_pairs={{0,15},{1,0},{2,1},{3,2},{4,3},{5,4},{6,5},{7,6},{8,7},{9,8},{10,9... | collective-permute-start | bytes 196616 | tf_op jit(solution)/shard_map/ppermute | solution.py:47
  145.3 7.6 %collective-permute-start.9 = (bf16[256,128]{1,0:T(8,128)(2,1)S(1)}, bf16[256,128]{1,0:T(8,128)(2,1)S(1)}, u32[]{:S(2)}, u32[]{:S(2)}) collective-permute-start(bf16[256,128]{1,0:T(8,128)(2,1)S(1)} %collective-permute-done.7), channel_id=1, source_target_pairs={{0,1},{1,2},{2,3},{3,4},{4,5},{5,6},{6,7},{7,8},{8,9},{9,10},{10,1... | collective-permute-start | bytes 196616 | tf_op jit(solution)/shard_map/ppermute | solution.py:42
  145.3 7.6 %collective-permute-start.10 = (bf16[256,128]{1,0:T(8,128)(2,1)S(1)}, bf16[256,128]{1,0:T(8,128)(2,1)S(1)}, u32[]{:S(2)}, u32[]{:S(2)}) collective-permute-start(bf16[256,128]{1,0:T(8,128)(2,1)S(1)} %collective-permute-done.8), channel_id=1, source_target_pairs={{0,15},{1,0},{2,1},{3,2},{4,3},{5,4},{6,5},{7,6},{8,7},{9,8},{10,9... | collective-permute-start | bytes 196616 | tf_op jit(solution)/shard_map/ppermute | solution.py:47
  152.9 7.6 %collective-permute-start.11 = (bf16[256,128]{1,0:T(8,128)(2,1)S(1)}, bf16[256,128]{1,0:T(8,128)(2,1)S(1)}, u32[]{:S(2)}, u32[]{:S(2)}) collective-permute-start(bf16[256,128]{1,0:T(8,128)(2,1)S(1)} %collective-permute-done.9), channel_id=1, source_target_pairs={{0,1},{1,2},{2,3},{3,4},{4,5},{5,6},{6,7},{7,8},{8,9},{9,10},{10,1... | collective-permute-start | bytes 196616 | tf_op jit(solution)/shard_map/ppermute | solution.py:42
  152.9 7.6 %collective-permute-start.12 = (bf16[256,128]{1,0:T(8,128)(2,1)S(1)}, bf16[256,128]{1,0:T(8,128)(2,1)S(1)}, u32[]{:S(2)}, u32[]{:S(2)}) collective-permute-start(bf16[256,128]{1,0:T(8,128)(2,1)S(1)} %collective-permute-done.10), channel_id=1, source_target_pairs={{0,15},{1,0},{2,1},{3,2},{4,3},{5,4},{6,5},{7,6},{8,7},{9,8},{10,9... | collective-permute-start | bytes 196616 | tf_op jit(solution)/shard_map/ppermute | solution.py:47
  160.5 7.6 %collective-permute-start.13 = (bf16[256,128]{1,0:T(8,128)(2,1)S(1)}, bf16[256,128]{1,0:T(8,128)(2,1)S(1)}, u32[]{:S(2)}, u32[]{:S(2)}) collective-permute-start(bf16[256,128]{1,0:T(8,128)(2,1)S(1)} %collective-permute-done.11), channel_id=1, source_target_pairs={{0,1},{1,2},{2,3},{3,4},{4,5},{5,6},{6,7},{7,8},{8,9},{9,10},{10,1... | collective-permute-start | bytes 196616 | tf_op jit(solution)/shard_map/ppermute | solution.py:42
  160.5 7.6 %collective-permute-start.14 = (bf16[256,128]{1,0:T(8,128)(2,1)S(1)}, bf16[256,128]{1,0:T(8,128)(2,1)S(1)}, u32[]{:S(2)}, u32[]{:S(2)}) collective-permute-start(bf16[256,128]{1,0:T(8,128)(2,1)S(1)} %collective-permute-done.12), channel_id=1, source_target_pairs={{0,15},{1,0},{2,1},{3,2},{4,3},{5,4},{6,5},{7,6},{8,7},{9,8},{10,9... | collective-permute-start | bytes 196616 | tf_op jit(solution)/shard_map/ppermute | solution.py:47
  168.0 7.8 %collective-permute-start.15 = (bf16[256,128]{1,0:T(8,128)(2,1)S(1)}, bf16[256,128]{1,0:T(8,128)(2,1)S(1)}, u32[]{:S(2)}, u32[]{:S(2)}) collective-permute-start(bf16[256,128]{1,0:T(8,128)(2,1)S(1)} %collective-permute-done.13), channel_id=1, source_target_pairs={{0,1},{1,2},{2,3},{3,4},{4,5},{5,6},{6,7},{7,8},{8,9},{9,10},{10,1... | collective-permute-start | bytes 196616 | tf_op jit(solution)/shard_map/ppermute | solution.py:42
  168.0 7.8 %collective-permute-start.16 = (bf16[256,128]{1,0:T(8,128)(2,1)S(1)}, bf16[256,128]{1,0:T(8,128)(2,1)S(1)}, u32[]{:S(2)}, u32[]{:S(2)}) collective-permute-start(bf16[256,128]{1,0:T(8,128)(2,1)S(1)} %collective-permute-done.14), channel_id=1, source_target_pairs={{0,15},{1,0},{2,1},{3,2},{4,3},{5,4},{6,5},{7,6},{8,7},{9,8},{10,9... | collective-permute-start | bytes 196616 | tf_op jit(solution)/shard_map/ppermute | solution.py:47
  175.8 7.6 %collective-permute-start.17 = (bf16[256,128]{1,0:T(8,128)(2,1)S(1)}, bf16[256,128]{1,0:T(8,128)(2,1)S(1)}, u32[]{:S(2)}, u32[]{:S(2)}) collective-permute-start(bf16[256,128]{1,0:T(8,128)(2,1)S(1)} %collective-permute-done.15), channel_id=1, source_target_pairs={{0,1},{1,2},{2,3},{3,4},{4,5},{5,6},{6,7},{7,8},{8,9},{9,10},{10,1... | collective-permute-start | bytes 196616 | tf_op jit(solution)/shard_map/ppermute | solution.py:42
Sparse Core Ops, SparseCore 0:
  16.1 82.7 reduce-scatter.1
